TPU v7x, 32 devices: a whole 2x2x4 slice. The times are simulated.
32 devices in a mesh: rep: 4 (over x, core), dev: 8 (over z, y).
Axes of the slice: x: 2, y: 2, z: 4, core: 2. Of those that a mesh axis runs over, the one named last changes fastest.
Arguments:
- group_weights: bfloat16 [4, 160, 128, 1024], P('rep', None, 'dev'), may hold values from -6 to 6
- owner: int32 [160], replicated, may hold values from 0 to 7, as said below
- start_weights: float32 [8, 40, 128, 1024], P('dev', None, None, 'rep'), may hold values from -6 to 6
- momentum: float32 [8, 40, 128, 1024], P('dev', None, None, 'rep'), may hold values from -6 to 6
- basis: float32 [64, 1024], replicated, may hold values from -1 to 1
- vec_groups: bfloat16 [4, 13, 1024], P('rep'), may hold values from -6 to 6
- vec_start: float32 [13, 1024], replicated, may hold values from -6 to 6
- vec_momentum: float32 [13, 1024], replicated, may hold values from -6 to 6
Outputs:
- new_start: float32 [8, 40, 128, 1024], P('dev', None, None, 'rep')
- new_momentum: float32 [8, 40, 128, 1024], P('dev', None, None, 'rep')
- returned: bfloat16 [160, 128, 1024], P(None, 'dev')
- vec_new: float32 [13, 1024], replicated
- vec_new_momentum: float32 [13, 1024], replicated
Inputs may be any that keep to these rules, and one draw needn't show every extreme that they name: `owner`: each index along dev owns at most 40 blocks, and some index owns exactly 40.
All inputs are finite; a program needn't handle non-finite values.
Results may differ from a plain program's by a relative error of at most 0.012.
Values may be sent and summed in bfloat16 or wider, within the bound.
No kernel may reach another device: no remote copies, remote signals or barrier semaphores. Data moves between devices by JAX's collectives and lax.ppermute only.
A program may use at most 128 MiB of HBM per device.

v0:
```python
import jax
import jax.numpy as jnp
from jax import lax
from jax.sharding import PartitionSpec as P

EMB_FIRST = 96
outer_rate = 0.7
outer_momentum = 0.9


def body(group_weights, owner, start_weights, momentum, basis, vec_groups, vec_start, vec_momentum):
    dev_count = lax.axis_size("dev")
    rep_count = lax.axis_size("rep")
    unit_count = owner.shape[0]
    slot_count = start_weights.shape[1]
    quarter = start_weights.shape[3]
    unit_ids = jnp.arange(unit_count, dtype=jnp.int32)
    same_owner = owner[:, None] == owner[None, :]
    earlier = unit_ids[None, :] < unit_ids[:, None]
    slot_of = jnp.sum((same_owner & earlier).astype(jnp.int32), axis=1)
    target = owner * slot_count + slot_of
    positions = jnp.arange(dev_count * slot_count, dtype=jnp.int32)
    placed = target[:, None] == positions[None, :]
    filled = jnp.any(placed, axis=0)
    source_unit = jnp.sum(jnp.where(placed, unit_ids[:, None], 0), axis=0)
    own_rows = group_weights[0]
    picked = jnp.take(own_rows, source_unit, axis=0)
    picked = jnp.where(filled[:, None, None], picked, jnp.zeros((), own_rows.dtype))
    arrived = lax.all_to_all(
        picked.reshape(dev_count, slot_count, own_rows.shape[1], own_rows.shape[2]),
        "dev",
        split_axis=0,
        concat_axis=2,
        tiled=True,
    )
    summed = lax.psum_scatter(
        arrived[0].astype(jnp.float32).astype(jnp.bfloat16), "rep", scatter_dimension=2, tiled=True
    ).astype(jnp.float32)
    group_mean = summed / rep_count
    start_rows = start_weights[0]
    momentum_rows = momentum[0]
    my_slots = lax.axis_index("dev") * slot_count + jnp.arange(slot_count, dtype=jnp.int32)
    own_placed = target[:, None] == my_slots[None, :]
    is_owned = jnp.any(own_placed, axis=0)
    is_embedding = jnp.any(own_placed & (unit_ids >= EMB_FIRST)[:, None], axis=0)
    change = start_rows - group_mean
    first_column = lax.axis_index("rep") * quarter
    basis_part = lax.dynamic_slice_in_dim(basis, first_column, quarter, 1)
    coeff_terms = jnp.einsum("sbq,kq->sbk", change, basis_part, precision=lax.Precision.HIGHEST)
    vec_terms = vec_groups[0].astype(jnp.float32)
    coeffs, vec_summed = (
        lax.psum(coeff_terms.astype(jnp.bfloat16), "rep").astype(jnp.float32),
        lax.psum(vec_terms.astype(jnp.bfloat16), "rep").astype(jnp.float32),
    )
    projected = jnp.einsum("sbk,kq->sbq", coeffs, basis_part, precision=lax.Precision.HIGHEST)
    outer_grad = jnp.where(is_embedding[:, None, None], projected, change)
    fresh_momentum = outer_momentum * momentum_rows + outer_grad
    fresh_start = start_rows - outer_rate * (outer_grad + outer_momentum * fresh_momentum)
    owned_mask = is_owned[:, None, None]
    new_momentum = jnp.where(owned_mask, fresh_momentum, momentum_rows)
    new_start = jnp.where(owned_mask, fresh_start, start_rows)
    rounded = fresh_start.astype(jnp.bfloat16)
    pieces = lax.all_to_all(rounded, "dev", split_axis=1, concat_axis=0, tiled=True)
    picked = jnp.take(pieces, target, axis=0)
    returned = lax.all_gather(picked, "rep", axis=2, tiled=True)
    vec_change = vec_start - vec_summed / rep_count
    vec_new_momentum = outer_momentum * vec_momentum + vec_change
    vec_new = vec_start - outer_rate * (vec_change + outer_momentum * vec_new_momentum)
    return (new_start[None], new_momentum[None], returned, vec_new, vec_new_momentum)


def solution(mesh):
    return jax.shard_map(
        body,
        mesh=mesh,
        in_specs=(
            P("rep", None, "dev", None),
            P(),
            P("dev", None, None, "rep"),
            P("dev", None, None, "rep"),
            P(),
            P("rep", None, None),
            P(),
            P(),
        ),
        out_specs=(
            P("dev", None, None, "rep"),
            P("dev", None, None, "rep"),
            P(None, "dev", None),
            P(),
            P(),
        ),
        check_vma=False,
    )
```

profile of v0, /device:TPU:0, one launch (start us, length us, event | category | flops | bytes accessed | tf_op | source)
XLA Modules:
  0.0 537.6 jit_solution(10734063896174378784)
XLA Ops:
  7.2 0.0 copy-start
  7.2 0.0 reduce-scatter.2.cloned.1.call-start
  7.2 0.9 convert_reduce_fusion
  8.2 0.7 compare_and_fusion.2
  8.9 0.1 select_reduce_fusion
  9.0 0.1 reduce_sum.24
  9.1 0.1 fusion.7
  9.2 0.1 broadcast_in_dim.85
  9.3 13.1 %gather_fusion = bf16[320,16,1024]{2,1,0:T(8,128)(2,1)} fusion(bf16[160,16,1024]{2,1,0:T(8,128)(2,1)} %bitcast.60, s32[1024]{0:T(1024)S(1)} %pad_clamp_fusion.1), kind=kCustom, calls=%fused_computation | custom fusion | bytes 20972800 | tf_op jit(solution)/shard_map/jit(_take)/gather | solution.py:27
  22.4 6.0 %select_select_fusion = bf16[8,40,16,1024]{3,2,1,0:T(8,128)(2,1)S(1)} fusion(bf16[8,40,16,1024]{3,2,1,0:T(8,128)(2,1)} %bitcast.59, pred[8,40]{1,0:T(8,128)(4,1)S(1)} %compare_and_fusion.1, pred[8,40]{1,0:T(8,128)(4,1)S(1)} %broadcast_in_dim.85), kind=kLoop, calls=%fused_computation.2 | loop fusion | flops 10485760 | bytes 20972160 | tf_op jit(solution)/shard_map/jit(_where)/select_n | solution.py:28
  28.3 235.2 %all_to_all.33 = bf16[8,40,16,1024]{3,2,1,0:T(8,128)(2,1)} all-to-all(bf16[8,40,16,1024]{3,2,1,0:T(8,128)(2,1)S(1)} %select_select_fusion), channel_id=1, replica_groups=mesh['rep'=4,'dev'=8] {'dev'}, dimensions={0} | all-to-all | bytes 20971520 | tf_op jit(solution)/shard_map/all_to_all | solution.py:29
  263.5 10.4 %copy.24 = bf16[1,40,8,16,1024]{4,3,2,1,0:T(8,128)(2,1)} copy(bf16[1,40,8,16,1024]{4,3,1,2,0:T(8,128)(2,1)} %bitcast.58) | data formatting | bytes 20971520 | tf_op jit(solution)/shard_map/all_to_all | solution.py:29
  274.0 0.0 reduce-scatter.2.cloned.1.call-update
  274.0 0.0 all-reduce.2.cloned.1.call-start
  274.0 84.4 %reduce-scatter.2.cloned.1.call-done = bf16[40,128,256]{2,1,0:T(8,128)(2,1)} async-done(((bf16[40,128,1024]{2,1,0:T(8,128)(2,1)}), bf16[40,128,256]{2,1,0:T(8,128)(2,1)}) %reduce-scatter.2.cloned.1.call-update) | async-done | bytes 2621456 | tf_op jit(solution)/shard_map/reduce_scatter | solution.py:36
  358.5 0.0 copy-done
  358.5 0.0 copy-start.1
  358.5 9.5 %fusion.6 = bf16[40,128,64]{1,2,0:T(8,128)(2,1)} fusion(f32[1,40,128,256]{3,2,1,0:T(8,128)} %param.10, bf16[40,128,256]{2,1,0:T(8,128)(2,1)} %reduce-scatter.2.cloned.1.call-done, f32[64,1024]{1,0:T(8,128)S(1)} %copy-done, s32[]{:T(128)S(6)} %select_n.58), kind=kOutput, calls=%fused_computation.14 | convolution fusion | flops 1010892800 | bytes 8585220 | tf_op jit(solution)/shard_map/sbq,kq->sbk/dot_general | solution.py:49
  368.0 0.0 all-reduce.2.cloned.1.call-update
  368.0 0.2 fusion.14
  368.2 33.7 %all-reduce.2.cloned.1.call-done = bf16[40,128,64]{1,2,0:T(8,128)(2,1)} async-done(((bf16[40,128,64]{1,2,0:T(8,128)(2,1)}), bf16[40,128,64]{1,2,0:T(8,128)(2,1)}) %all-reduce.2.cloned.1.call-update) | async-done | bytes 655376 | tf_op jit(solution)/shard_map/psum | solution.py:52
  401.9 0.0 copy-done.1
  401.9 10.2 %fusion.1 = (f32[1,40,128,256]{3,2,1,0:T(8,128)}, f32[1,40,128,256]{3,2,1,0:T(8,128)}, bf16[40,128,256]{2,1,0:T(8,128)(2,1)S(1)}) fusion(f32[1,40,128,256]{3,2,1,0:T(8,128)} %param.11, bf16[40,128,256]{2,1,0:T(8,128)(2,1)S(1)} %copy-done.1, f32[1,40,128,256]{3,2,1,0:T(8,128)} %param.10, pred[40]{0:T(512)(128)(4,1)S(1)} %get-tuple-element.5, ...), kind=kOutput, calls=%fused_computation.6 | convolution fusion | flops 1023672320 | bytes 26936324 | tf_op jit(solution)/shard_map/sbk,kq->sbq/dot_general | solution.py:55
  412.1 3.0 copy.25
  415.1 5.5 %all-to-all-start.1 = ((bf16[40,128,256]{2,0,1:T(8,128)(2,1)}), bf16[40,128,256]{2,0,1:T(8,128)(2,1)S(1)}, u32[]{:S(2)}, u32[]{:S(2)}) async-start(bf16[40,128,256]{2,0,1:T(8,128)(2,1)} %copy.25), calls=%async_computation.2 | async-start | bytes 5242880 | tf_op jit(solution)/shard_map/all_to_all | solution.py:63
  420.6 0.0 all-gather.2.cloned.1.call-start
  420.7 58.5 %all-to-all-done.1 = bf16[40,128,256]{2,0,1:T(8,128)(2,1)S(1)} async-done(((bf16[40,128,256]{2,0,1:T(8,128)(2,1)}), bf16[40,128,256]{2,0,1:T(8,128)(2,1)S(1)}, u32[]{:S(2)}, u32[]{:S(2)}) %all-to-all-start.1) | async-done | bytes 2621472 | tf_op jit(solution)/shard_map/all_to_all | solution.py:63
  479.2 0.0 copy-start.4
  479.2 0.0 copy-start.2
  479.2 0.0 copy-start.3
  479.2 2.1 copy.27
  481.2 2.6 gather_fusion.1
  483.8 1.3 broadcast_select_fusion
  485.1 0.0 all-gather.2.cloned.1.call-update
  485.1 0.0 copy-done.4
  485.2 10.3 %psum.15 = bf16[13,1024]{1,0:T(8,128)(2,1)S(1)} all-reduce(bf16[13,1024]{1,0:T(8,128)(2,1)S(1)} %bitcast.63), channel_id=1, replica_groups=mesh['rep'=4,'dev'=8] {'rep'}, use_global_device_ids=true, to_apply=%region_7.8 | all-reduce | flops 13312 | bytes 53248 | tf_op jit(solution)/shard_map/psum | solution.py:53
  495.4 0.0 copy-done.2
  495.4 0.0 copy-done.3
  495.5 0.7 multiply_subtract_fusion
  496.1 28.9 %all-gather.2.cloned.1.call-done = bf16[160,16,1024]{2,1,0:T(8,128)(2,1)} async-done(((bf16[160,16,256]{2,1,0:T(8,128)(2,1)}), bf16[160,16,1024]{2,1,0:T(8,128)(2,1)}) %all-gather.2.cloned.1.call-update) | async-done | bytes 5242896 | tf_op jit(solution)/shard_map/all_gather | solution.py:65
  525.1 6.0 %copy.31 = bf16[160,16,1024]{2,1,0:T(8,128)(2,1)} copy(bf16[160,16,1024]{2,1,0:T(8,128)(2,1)} %all-gather.2.cloned.1.call-done) | data formatting | bytes 10485760
  (6 shorter events, 0.0 us)
Async XLA Ops:
  7.2 351.3 %copy-start = (f32[64,1024]{1,0:T(8,128)S(1)}, f32[64,1024]{1,0:T(8,128)}, u32[]{:S(2)}) copy-start(f32[64,1024]{1,0:T(8,128)} %param.12) | copy-start | bytes 786436
  7.2 351.3 %reduce-scatter.2.cloned.1.call-start = ((), (), s32[]{:S(2)}) async-start(), calls=%async_computation.3 | async-start | bytes 13107200 | tf_op jit(solution)/shard_map/reduce_scatter | solution.py:36
  274.0 128.0 %all-reduce.2.cloned.1.call-start = ((), (), s32[]{:S(2)}) async-start(), calls=%async_computation.4 | async-start | bytes 1310720 | tf_op jit(solution)/shard_map/psum | solution.py:52
  358.5 43.5 %copy-start.1 = (bf16[40,128,256]{2,1,0:T(8,128)(2,1)S(1)}, bf16[40,128,256]{2,1,0:T(8,128)(2,1)}, u32[]{:S(2)}) copy-start(bf16[40,128,256]{2,1,0:T(8,128)(2,1)} %reduce-scatter.2.cloned.1.call-done) | copy-start | bytes 7864324
  415.1 64.1 %all-to-all-start.1 = ((bf16[40,128,256]{2,0,1:T(8,128)(2,1)}), bf16[40,128,256]{2,0,1:T(8,128)(2,1)S(1)}, u32[]{:S(2)}, u32[]{:S(2)}) async-start(bf16[40,128,256]{2,0,1:T(8,128)(2,1)} %copy.25), calls=%async_computation.2 | async-start | bytes 5242880 | tf_op jit(solution)/shard_map/all_to_all | solution.py:63
  420.6 104.5 %all-gather.2.cloned.1.call-start = ((), (), s32[]{:S(2)}) async-start(), calls=%async_computation.5 | async-start | bytes 6553600 | tf_op jit(solution)/shard_map/all_gather | solution.py:65
  479.2 6.0 %copy-start.4 = (bf16[1,13,1024]{2,1,0:T(8,128)(2,1)S(1)}, bf16[1,13,1024]{2,1,0:T(8,128)(2,1)}, u32[]{:S(2)}) copy-start(bf16[1,13,1024]{2,1,0:T(8,128)(2,1)} %param.13) | copy-start | bytes 79876
  479.2 16.3 %copy-start.2 = (f32[13,1024]{1,0:T(8,128)S(1)}, f32[13,1024]{1,0:T(8,128)}, u32[]{:S(2)}) copy-start(f32[13,1024]{1,0:T(8,128)} %param.14) | copy-start | bytes 159748
  479.2 16.3 %copy-start.3 = (f32[13,1024]{1,0:T(8,128)S(1)}, f32[13,1024]{1,0:T(8,128)}, u32[]{:S(2)}) copy-start(f32[13,1024]{1,0:T(8,128)} %param.15) | copy-start | bytes 159748
Sparse Core Ops, SparseCore 0:
  274.1 84.3 reduce-scatter.1
  368.1 33.7 all-reduce.1
  485.3 39.7 all-gather.1
where the time goes:
time: 538 us
  blocking collectives  245 us (46%)
  waiting for transfers between devices  206 us (38%)
  local copies, waits for them, and re-layouts  37.2 us (7%)
  matrix products  19.7 us (4%)
  between operations  13.9 us (3%)
  other arithmetic  10 us (2%)
  starting transfers between devices  5.63 us (1%)
    all_to_all x1, blocking collectives, body(): lax.all_to_all(picked.reshape(dev_count, slot_count, own_rows.shape[1], o...  235 us
    reduce_scatter x1, waiting for transfers between devices, body(): lax.psum_scatter(arrived[0].astype(jnp.float32).astype(jnp.bfloat16), 're...  84.4 us
    all_to_all x1, waiting for transfers between devices, body(): lax.all_to_all(rounded, 'dev', split_axis=1, concat_axis=0, tiled=True)  58.5 us
    psum x1, waiting for transfers between devices, body(): lax.psum(coeff_terms.astype(jnp.bfloat16), 'rep').astype(jnp.float32)  33.7 us
    all_gather x1, waiting for transfers between devices, body(): returned = lax.all_gather(picked, 'rep', axis=2, tiled=True)  28.9 us
    gather x1, local copies, waits for them, and re-layouts, body(): picked = jnp.take(own_rows, source_unit, axis=0)  13.1 us
  transfers between devices with their start and end apart: 4, of which 4 were waited for; matrix products, arithmetic and copies ran while one was open for 0% of the time, Pallas kernels for 0%

commit v1 on v0

--- a/solution.py
+++ b/solution.py
@@ -1,3 +1,4 @@
+import functools
 import jax
 import jax.numpy as jnp
 from jax import lax
@@ -6,6 +7,21 @@
 EMB_FIRST = 96
 outer_rate = 0.7
 outer_momentum = 0.9
+
+
+def choose_views(payload, along_axis):
+    total_devices = jax.lax.axis_size(along_axis)
+    block_next = payload
+    row_list = [block_next]
+    view_out = [(dd - 1, dd) for dd in range(1, total_devices)] + [(total_devices - 1, 0)]
+    for _ in tuple(range(total_devices - 1)):
+        block_next = jax.lax.ppermute(block_next, along_axis, view_out)
+        row_list += [block_next]
+    r_now = jnp.concatenate([*reversed(row_list)], 2)
+    return jnp.roll(r_now, (jax.lax.axis_index(along_axis) + 1) * block_next.shape[2], 2)
+
+
+_drive_positions = functools.partial(choose_views, along_axis="rep")
 
 
 def body(group_weights, owner, start_weights, momentum, basis, vec_groups, vec_start, vec_momentum):
@@ -62,7 +78,7 @@
     rounded = fresh_start.astype(jnp.bfloat16)
     pieces = lax.all_to_all(rounded, "dev", split_axis=1, concat_axis=0, tiled=True)
     picked = jnp.take(pieces, target, axis=0)
-    returned = lax.all_gather(picked, "rep", axis=2, tiled=True)
+    returned = _drive_positions(picked)
     vec_change = vec_start - vec_summed / rep_count
     vec_new_momentum = outer_momentum * vec_momentum + vec_change
     vec_new = vec_start - outer_rate * (vec_change + outer_momentum * vec_new_momentum)

time: 538 us -> 559 us (1.039)
  blocking collectives: 245 us -> 258 us
    ppermute x0 -> x3, waiting for transfers between devices: none -> 34.2 us  [choose_views(): block_next = jax.lax.ppermute(block_next, along_axis, view_out)]
    all_gather x1 -> x0, waiting for transfers between devices: 28.9 us -> none  [body(): returned = lax.all_gather(picked, 'rep', axis=2, tiled=True)]
    psum x1, blocking collectives: 10.3 us -> 22.7 us  [body(): lax.psum(vec_terms.astype(jnp.bfloat16), 'rep').astype(jnp.float32)]
  transfers between devices with their start and end apart: 4 -> 6, of which waited for: 4 -> 5; matrix products, arithmetic and copies ran while one was open for 0% -> 0% of each run, Pallas kernels for 0% -> 0%
where the time goes in v1:
time: 559 us
  blocking collectives  258 us (46%)
  waiting for transfers between devices  211 us (38%)
  local copies, waits for them, and re-layouts  40.5 us (7%)
  matrix products  19.7 us (4%)
  between operations  14.2 us (3%)
  other arithmetic  9.61 us (2%)
  starting transfers between devices  5.84 us (1%)
    all_to_all x1, blocking collectives, body(): lax.all_to_all(picked.reshape(dev_count, slot_count, own_rows.shape[1], o...  235 us
    reduce_scatter x1, waiting for transfers between devices, body(): lax.psum_scatter(arrived[0].astype(jnp.float32).astype(jnp.bfloat16), 're...  84.4 us
    all_to_all x1, waiting for transfers between devices, body(): lax.all_to_all(rounded, 'dev', split_axis=1, concat_axis=0, tiled=True)  58.5 us
    ppermute x3, waiting for transfers between devices, choose_views(): block_next = jax.lax.ppermute(block_next, along_axis, view_out)  34.2 us
    psum x1, waiting for transfers between devices, body(): lax.psum(coeff_terms.astype(jnp.bfloat16), 'rep').astype(jnp.float32)  33.7 us
    psum x1, blocking collectives, body(): lax.psum(vec_terms.astype(jnp.bfloat16), 'rep').astype(jnp.float32)  22.7 us
    gather x1, local copies, waits for them, and re-layouts, body(): picked = jnp.take(own_rows, source_unit, axis=0)  13.1 us
  transfers between devices with their start and end apart: 6, of which 5 were waited for; matrix products, arithmetic and copies ran while one was open for 0% of the time, Pallas kernels for 0%

profile of v1, /device:TPU:0, one launch (start us, length us, event | category | flops | bytes accessed | tf_op | source)
XLA Modules:
  0.0 558.7 jit_solution(5766408001948646869)
XLA Ops:
  7.2 0.0 copy-start
  7.2 0.0 reduce-scatter.2.cloned.1.call-start
  7.2 0.9 convert_reduce_fusion
  8.2 0.7 compare_and_fusion.2
  8.9 0.1 select_reduce_fusion
  9.0 0.1 reduce_sum.24
  9.1 0.1 fusion.7
  9.2 0.1 broadcast_in_dim.85
  9.3 13.1 %gather_fusion = bf16[320,16,1024]{2,1,0:T(8,128)(2,1)} fusion(bf16[160,16,1024]{2,1,0:T(8,128)(2,1)} %bitcast.60, s32[1024]{0:T(1024)S(1)} %pad_clamp_fusion.1), kind=kCustom, calls=%fused_computation | custom fusion | bytes 20972800 | tf_op jit(solution)/shard_map/jit(_take)/gather | solution.py:43
  22.4 6.0 %select_select_fusion = bf16[8,40,16,1024]{3,2,1,0:T(8,128)(2,1)S(1)} fusion(bf16[8,40,16,1024]{3,2,1,0:T(8,128)(2,1)} %bitcast.59, pred[8,40]{1,0:T(8,128)(4,1)S(1)} %compare_and_fusion.1, pred[8,40]{1,0:T(8,128)(4,1)S(1)} %broadcast_in_dim.85), kind=kLoop, calls=%fused_computation.2 | loop fusion | flops 10485760 | bytes 20972160 | tf_op jit(solution)/shard_map/jit(_where)/select_n | solution.py:44
  28.3 235.2 %all_to_all.33 = bf16[8,40,16,1024]{3,2,1,0:T(8,128)(2,1)} all-to-all(bf16[8,40,16,1024]{3,2,1,0:T(8,128)(2,1)S(1)} %select_select_fusion), channel_id=1, replica_groups=mesh['rep'=4,'dev'=8] {'dev'}, dimensions={0} | all-to-all | bytes 20971520 | tf_op jit(solution)/shard_map/all_to_all | solution.py:45
  263.5 10.4 %copy.24 = bf16[1,40,8,16,1024]{4,3,2,1,0:T(8,128)(2,1)} copy(bf16[1,40,8,16,1024]{4,3,1,2,0:T(8,128)(2,1)} %bitcast.58) | data formatting | bytes 20971520 | tf_op jit(solution)/shard_map/all_to_all | solution.py:45
  274.0 0.0 reduce-scatter.2.cloned.1.call-update
  274.0 0.0 all-reduce.2.cloned.1.call-start
  274.0 84.4 %reduce-scatter.2.cloned.1.call-done = bf16[40,128,256]{2,1,0:T(8,128)(2,1)} async-done(((bf16[40,128,1024]{2,1,0:T(8,128)(2,1)}), bf16[40,128,256]{2,1,0:T(8,128)(2,1)}) %reduce-scatter.2.cloned.1.call-update) | async-done | bytes 2621456 | tf_op jit(solution)/shard_map/reduce_scatter | solution.py:52
  358.5 0.0 copy-done
  358.5 9.5 %fusion.6 = bf16[40,128,64]{1,2,0:T(8,128)(2,1)} fusion(f32[1,40,128,256]{3,2,1,0:T(8,128)} %param.10, bf16[40,128,256]{2,1,0:T(8,128)(2,1)} %reduce-scatter.2.cloned.1.call-done, f32[64,1024]{1,0:T(8,128)S(1)} %copy-done, s32[]{:T(128)S(6)} %select_n.71), kind=kOutput, calls=%fused_computation.14 | convolution fusion | flops 1010892800 | bytes 8585220 | tf_op jit(solution)/shard_map/sbq,kq->sbk/dot_general | solution.py:65
  368.0 0.0 all-reduce.2.cloned.1.call-update
  368.0 0.2 fusion.14
  368.2 33.7 %all-reduce.2.cloned.1.call-done = bf16[40,128,64]{1,2,0:T(8,128)(2,1)} async-done(((bf16[40,128,64]{1,2,0:T(8,128)(2,1)}), bf16[40,128,64]{1,2,0:T(8,128)(2,1)}) %all-reduce.2.cloned.1.call-update) | async-done | bytes 655376 | tf_op jit(solution)/shard_map/psum | solution.py:68
  401.9 0.0 copy-done.1
  401.9 10.2 %fusion.1 = (f32[1,40,128,256]{3,2,1,0:T(8,128)}, f32[1,40,128,256]{3,2,1,0:T(8,128)}, bf16[40,128,256]{2,1,0:T(8,128)(2,1)S(1)}) fusion(f32[1,40,128,256]{3,2,1,0:T(8,128)} %param.11, bf16[40,128,256]{2,1,0:T(8,128)(2,1)S(1)} %copy-done.1, f32[1,40,128,256]{3,2,1,0:T(8,128)} %param.10, pred[40]{0:T(512)(128)(4,1)S(1)} %get-tuple-element.5, ...), kind=kOutput, calls=%fused_computation.6 | convolution fusion | flops 1023672320 | bytes 26936324 | tf_op jit(solution)/shard_map/sbk,kq->sbq/dot_general | solution.py:71
  412.1 3.0 copy.25
  415.1 5.7 %all-to-all-start.1 = ((bf16[40,128,256]{2,0,1:T(8,128)(2,1)}), bf16[40,128,256]{2,0,1:T(8,128)(2,1)S(1)}, u32[]{:S(2)}, u32[]{:S(2)}) async-start(bf16[40,128,256]{2,0,1:T(8,128)(2,1)} %copy.25), calls=%async_computation.2 | async-start | bytes 5242880 | tf_op jit(solution)/shard_map/all_to_all | solution.py:79
  420.8 58.5 %all-to-all-done.1 = bf16[40,128,256]{2,0,1:T(8,128)(2,1)S(1)} async-done(((bf16[40,128,256]{2,0,1:T(8,128)(2,1)}), bf16[40,128,256]{2,0,1:T(8,128)(2,1)S(1)}, u32[]{:S(2)}, u32[]{:S(2)}) %all-to-all-start.1) | async-done | bytes 2621472 | tf_op jit(solution)/shard_map/all_to_all | solution.py:79
  479.4 2.1 copy.27
  481.4 2.6 gather_fusion.1
  484.0 0.2 broadcast_select_fusion
  484.2 0.1 collective-permute-start
  484.3 17.0 %collective-permute-done = bf16[160,16,256]{2,1,0:T(8,128)(2,1)S(1)} collective-permute-done((bf16[160,16,256]{2,1,0:T(8,128)(2,1)S(1)}, bf16[160,16,256]{2,1,0:T(8,128)(2,1)S(1)}, u32[]{:S(2)}, u32[]{:S(2)}) %collective-permute-start) | collective-permute-done | bytes 1310752 | tf_op jit(solution)/shard_map/ppermute | solution.py:18
  501.3 0.0 collective-permute-start.1
  501.3 17.1 %collective-permute-done.1 = bf16[160,16,256]{2,1,0:T(8,128)(2,1)} collective-permute-done((bf16[160,16,256]{2,1,0:T(8,128)(2,1)S(1)}, bf16[160,16,256]{2,1,0:T(8,128)(2,1)}, u32[]{:S(2)}, u32[]{:S(2)}) %collective-permute-start.1) | collective-permute-done | bytes 1310752 | tf_op jit(solution)/shard_map/ppermute | solution.py:18
  518.5 0.0 collective-permute-start.2
  518.5 0.0 copy-done.4
  518.5 22.7 %psum.15 = bf16[13,1024]{1,0:T(8,128)(2,1)S(1)} all-reduce(bf16[13,1024]{1,0:T(8,128)(2,1)S(1)} %bitcast.63), channel_id=1, replica_groups=mesh['rep'=4,'dev'=8] {'rep'}, use_global_device_ids=true, to_apply=%region_7.8 | all-reduce | flops 13312 | bytes 53248 | tf_op jit(solution)/shard_map/psum | solution.py:69
  541.1 0.0 copy-done.2
  541.1 0.0 copy-done.3
  541.2 0.7 multiply_subtract_fusion
  541.8 0.0 collective-permute-done.2
  541.8 1.5 constant_dynamic-update-slice_fusion.7
  543.3 1.5 constant_dynamic-update-slice_fusion.6
  544.8 0.2 constant_dynamic-update-slice_fusion.5
  545.0 0.3 constant_dynamic-update-slice_fusion.4
  545.4 1.5 constant_dynamic-update-slice_fusion.3
  546.9 1.5 constant_dynamic-update-slice_fusion.2
  548.4 0.2 constant_dynamic-update-slice_fusion.1
  548.5 0.3 constant_dynamic-update-slice_fusion
  548.9 2.9 constant_dynamic-slice_fusion
  (10 shorter events, 0.1 us)
Async XLA Ops:
  7.2 351.3 %copy-start = (f32[64,1024]{1,0:T(8,128)S(1)}, f32[64,1024]{1,0:T(8,128)}, u32[]{:S(2)}) copy-start(f32[64,1024]{1,0:T(8,128)} %param.12) | copy-start | bytes 786436
  7.2 351.3 %reduce-scatter.2.cloned.1.call-start = ((), (), s32[]{:S(2)}) async-start(), calls=%async_computation.3 | async-start | bytes 13107200 | tf_op jit(solution)/shard_map/reduce_scatter | solution.py:52
  274.0 127.9 %all-reduce.2.cloned.1.call-start = ((), (), s32[]{:S(2)}) async-start(), calls=%async_computation.4 | async-start | bytes 1310720 | tf_op jit(solution)/shard_map/psum | solution.py:68
  358.5 43.5 %copy-start.1 = (bf16[40,128,256]{2,1,0:T(8,128)(2,1)S(1)}, bf16[40,128,256]{2,1,0:T(8,128)(2,1)}, u32[]{:S(2)}) copy-start(bf16[40,128,256]{2,1,0:T(8,128)(2,1)} %reduce-scatter.2.cloned.1.call-done) | copy-start | bytes 7864324
  415.1 64.3 %all-to-all-start.1 = ((bf16[40,128,256]{2,0,1:T(8,128)(2,1)}), bf16[40,128,256]{2,0,1:T(8,128)(2,1)S(1)}, u32[]{:S(2)}, u32[]{:S(2)}) async-start(bf16[40,128,256]{2,0,1:T(8,128)(2,1)} %copy.25), calls=%async_computation.2 | async-start | bytes 5242880 | tf_op jit(solution)/shard_map/all_to_all | solution.py:79
  479.4 39.1 %copy-start.4 = (bf16[1,13,1024]{2,1,0:T(8,128)(2,1)S(1)}, bf16[1,13,1024]{2,1,0:T(8,128)(2,1)}, u32[]{:S(2)}) copy-start(bf16[1,13,1024]{2,1,0:T(8,128)(2,1)} %param.13) | copy-start | bytes 79876
  479.4 61.8 %copy-start.2 = (f32[13,1024]{1,0:T(8,128)S(1)}, f32[13,1024]{1,0:T(8,128)}, u32[]{:S(2)}) copy-start(f32[13,1024]{1,0:T(8,128)} %param.14) | copy-start | bytes 159748
  479.4 61.8 %copy-start.3 = (f32[13,1024]{1,0:T(8,128)S(1)}, f32[13,1024]{1,0:T(8,128)}, u32[]{:S(2)}) copy-start(f32[13,1024]{1,0:T(8,128)} %param.15) | copy-start | bytes 159748
  484.2 17.1 %collective-permute-start = (bf16[160,16,256]{2,1,0:T(8,128)(2,1)S(1)}, bf16[160,16,256]{2,1,0:T(8,128)(2,1)S(1)}, u32[]{:S(2)}, u32[]{:S(2)}) collective-permute-start(bf16[160,16,256]{2,1,0:T(8,128)(2,1)S(1)} %broadcast_select_fusion), channel_id=1, source_target_pairs={{0,8},{8,16},{16,24},{24,0},{1,9},{9,17},{17,25},{25,1},{2,10},{10... | collective-permute-start | bytes 3932168 | tf_op jit(solution)/shard_map/ppermute | solution.py:18
  501.3 17.1 %collective-permute-start.1 = (bf16[160,16,256]{2,1,0:T(8,128)(2,1)S(1)}, bf16[160,16,256]{2,1,0:T(8,128)(2,1)}, u32[]{:S(2)}, u32[]{:S(2)}) collective-permute-start(bf16[160,16,256]{2,1,0:T(8,128)(2,1)S(1)} %collective-permute-done), channel_id=1, source_target_pairs={{0,8},{8,16},{16,24},{24,0},{1,9},{9,17},{17,25},{25,1},{2,10},{10... | collective-permute-start | bytes 3932168 | tf_op jit(solution)/shard_map/ppermute | solution.py:18
  518.5 23.4 %collective-permute-start.2 = (bf16[160,16,256]{2,1,0:T(8,128)(2,1)}, bf16[160,16,256]{2,1,0:T(8,128)(2,1)}, u32[]{:S(2)}, u32[]{:S(2)}) collective-permute-start(bf16[160,16,256]{2,1,0:T(8,128)(2,1)} %collective-permute-done.1), channel_id=1, source_target_pairs={{0,8},{8,16},{16,24},{24,0},{1,9},{9,17},{17,25},{25,1},{2,10},{10... | collective-permute-start | bytes 3932168 | tf_op jit(solution)/shard_map/ppermute | solution.py:18
Sparse Core Ops, SparseCore 0:
  274.1 84.3 reduce-scatter.1
  368.1 33.7 all-reduce.1
